TPU v7x, 512 devices: a whole 4x8x8 slice. The times are simulated.
512 devices in a mesh: tm: 32 (over x, y), space: 16 (over z, core).
Axes of the slice: x: 4, y: 8, z: 8, core: 2. Of those that a mesh axis runs over, the one named last changes fastest.
Arguments:
- data: bfloat16 [4096, 131072], P('tm', 'space'), may hold values from -40 to 40
- weights: float32 [131072], P('space'), may hold values from 1 to 30
- freqs: int32 [32], replicated, may hold values from 0 to 32, as said below
- n_keep: int32 [32], replicated, may hold values from 1 to 64, as said below
Outputs:
- mode_field: bfloat16 [32, 2, 64, 131072], P('tm', None, None, 'space')
- energy: float32 [32], P('tm')
Inputs may be any that keep to these rules, and one draw needn't show every extreme that they name: `freqs`: 32 distinct bins, among them 0 and 32, in an order drawn from the seed. `n_keep`: some frequency keeps all 64 columns and another keeps one.
All inputs are finite; a program needn't handle non-finite values.
Results may differ from a plain program's by a relative error of at most 0.0052.
Values may be sent and summed in bfloat16 or wider, within the bound.
No kernel may reach another device: no remote copies, remote signals or barrier semaphores. Data moves between devices by JAX's collectives and lax.ppermute only.
A program may use at most 64 MiB of HBM per device.

v0:
```python
import jax
import jax.numpy as jnp
from jax import lax
from jax.sharding import PartitionSpec as P

NT = 64
NS_STEPS = 4


def spectra_table(freqs):
    time_int = jnp.arange(NT, dtype=jnp.int32)
    time_float = time_int.astype(jnp.float32)
    window = 0.5 - 0.5 * jnp.cos(2.0 * jnp.pi * time_float / NT)
    norm = jnp.sqrt(jnp.sum(window * window))
    wrapped = freqs[:, None] * time_int[None, :] % NT
    phase_angle = 2.0 * jnp.pi * wrapped.astype(jnp.float32) / NT
    real_rows = window[None, :] * jnp.cos(phase_angle) / norm
    imag_rows = -window[None, :] * jnp.sin(phase_angle) / norm
    return jnp.concatenate([real_rows, imag_rows], axis=0).astype(jnp.bfloat16)


def transform_blocks(dft_table, snapshots, freq_count):
    block_count = snapshots.shape[0] // NT
    point_count = snapshots.shape[1]
    block_view = snapshots.reshape(block_count, NT, point_count)
    spectra = jnp.einsum("rt,btp->rbp", dft_table, block_view, preferred_element_type=jnp.float32)
    return spectra.reshape(2, freq_count, block_count, point_count)


def gram_terms(spectra, point_weights, total_points):
    spectra_re = spectra[0]
    spectra_im = spectra[1]
    stacked = jnp.concatenate([spectra_re, spectra_im], axis=1)
    square = (
        jnp.einsum(
            "fip,fjp->fij",
            stacked * point_weights[None, None, :],
            stacked,
            precision=lax.Precision.HIGHEST,
        )
        / total_points
    )
    return square


def unfold_terms(summed, block_count):
    g_one = summed[:, :block_count, :block_count] + summed[:, block_count:, block_count:]
    g_two = summed[:, :block_count, block_count:] - summed[:, block_count:, :block_count]
    return (g_one, g_two)


def inverse_root(embedded):
    size_two = embedded.shape[1]
    frobenius = jnp.sqrt(jnp.sum(embedded * embedded, axis=(1, 2)) + 1e-06)
    identity = jnp.broadcast_to(jnp.eye(size_two, dtype=jnp.float32), embedded.shape)
    current = embedded / frobenius[:, None, None]
    result = identity
    for sweep in range(NS_STEPS):
        factor = 1.5 * identity - 0.5 * jnp.einsum(
            "fij,fjk->fik", result, current, precision=lax.Precision.HIGHEST
        )
        current = jnp.einsum("fij,fjk->fik", current, factor, precision=lax.Precision.HIGHEST)
        result = jnp.einsum("fij,fjk->fik", factor, result, precision=lax.Precision.HIGHEST)
    return result


def finish_modes(spectra, summed, kept_counts, block_count):
    g_one, g_two = unfold_terms(summed, block_count)
    embedded = jnp.concatenate(
        [jnp.concatenate([g_one, -g_two], axis=2), jnp.concatenate([g_two, g_one], axis=2)], axis=1
    )
    inv_root = inverse_root(embedded)
    z_top = inv_root[:, :block_count, :block_count]
    z_low = inv_root[:, block_count:, :block_count]
    spectra_re = spectra[0]
    spectra_im = spectra[1]
    mode_re = jnp.einsum(
        "fij,fip->fjp", z_top, spectra_re, precision=lax.Precision.HIGHEST
    ) - jnp.einsum("fij,fip->fjp", z_low, spectra_im, precision=lax.Precision.HIGHEST)
    mode_im = jnp.einsum(
        "fij,fip->fjp", z_top, spectra_im, precision=lax.Precision.HIGHEST
    ) + jnp.einsum("fij,fip->fjp", z_low, spectra_re, precision=lax.Precision.HIGHEST)
    kept_mask = jnp.arange(block_count, dtype=jnp.int32)[None, :] < kept_counts[:, None]
    both_parts = jnp.stack([mode_re, mode_im], axis=1)
    mode_field = jnp.where(
        kept_mask[:, None, :, None], both_parts, jnp.zeros_like(both_parts)
    ).astype(jnp.bfloat16)
    energy = jnp.trace(g_one, axis1=1, axis2=2) / block_count
    return (mode_field, energy)


def shards(data, weights, freqs, n_keep):
    tm_count = lax.axis_size("tm")
    freq_count = freqs.shape[0]
    points_here = data.shape[1]
    total_points = points_here * lax.axis_size("space")
    block_count = data.shape[0] // NT * tm_count
    dft_table = spectra_table(freqs)
    spectra = transform_blocks(dft_table, data, freq_count)
    regrouped = lax.all_to_all(spectra, "tm", split_axis=1, concat_axis=2, tiled=True)
    partial_value = gram_terms(regrouped, weights, total_points)
    summed = lax.psum(partial_value, "space")
    kept_counts = lax.dynamic_slice_in_dim(n_keep, lax.axis_index("tm"), 1)
    mode_field, energy = finish_modes(regrouped, summed, kept_counts, block_count)
    return (mode_field, energy)


def solution(mesh):
    placed = (P("tm", "space"), P("space"), P(), P())
    return jax.shard_map(
        shards,
        mesh=mesh,
        in_specs=placed,
        out_specs=(P("tm", None, None, "space"), P("tm")),
        check_vma=False,
    )
```

profile of v0, /device:TPU:1, one launch (start us, length us, event | category | flops | bytes accessed | tf_op | source)
XLA Modules:
  0.0 300.4 jit_solution(1019790081844584022)
XLA Ops:
  7.2 0.0 copy-start
  7.2 0.7 multiply_reduce_fusion
  8.6 0.8 divide_convert_fusion.1
  9.4 0.0 copy-done
  9.4 0.7 fusion.36
  10.1 5.2 %copy.10 = f32[2,32,2,8192]{3,2,0,1:T(2,128)} copy(f32[2,32,2,8192]{3,1,2,0:T(8,128)S(1)} %fusion.36) | data formatting | bytes 8388608 | tf_op jit(solution)/shard_map/rt,btp->rbp/dot_general | solution.py:26
  15.3 0.0 copy-start.4
  15.3 10.7 %all-to-all-start = ((f32[2,32,2,8192]{3,2,0,1:T(2,128)}), f32[2,32,2,8192]{3,2,0,1:T(2,128)}, u32[]{:S(2)}, u32[]{:S(2)}) async-start(f32[2,32,2,8192]{3,2,0,1:T(2,128)} %copy.10), calls=%async_computation | async-start | bytes 8388608 | tf_op jit(solution)/shard_map/all_to_all | solution.py:100
  26.1 0.0 all-reduce.2.cloned.1.call-start
  26.1 0.0 copy-done.4
  26.1 0.6 dynamic_slice.3
  26.7 92.0 %all-to-all-done = f32[2,32,2,8192]{3,2,0,1:T(2,128)} async-done(((f32[2,32,2,8192]{3,2,0,1:T(2,128)}), f32[2,32,2,8192]{3,2,0,1:T(2,128)}, u32[]{:S(2)}, u32[]{:S(2)}) %all-to-all-start) | async-done | bytes 4194336 | tf_op jit(solution)/shard_map/all_to_all | solution.py:100
  118.7 4.8 %fusion.35 = (f32[1,32,2,8192]{3,2,0,1:T(2,128)}, f32[1,32,2,8192]{3,2,0,1:T(2,128)}) fusion(f32[2,32,2,8192]{3,2,0,1:T(2,128)} %all-to-all-done), kind=kLoop, calls=%fused_computation.61 | loop fusion | bytes 8388608 | tf_op jit(solution)/shard_map/slice | solution.py:31
  123.5 5.2 %squeeze.8 = f32[1,64,8192]{2,0,1:T(1,128)} reshape(f32[1,32,2,8192]{3,2,0,1:T(2,128)} %get-tuple-element.6) | data formatting | bytes 4194304 | tf_op jit(solution)/shard_map/squeeze | solution.py:31
  128.7 3.7 %concatenate.53 = f32[64,8192]{1,0:T(8,128)} reshape(f32[1,32,2,8192]{3,2,0,1:T(2,128)} %get-tuple-element.6) | data formatting | bytes 4194304 | tf_op jit(solution)/shard_map/concatenate | solution.py:33
  132.4 5.2 %squeeze.9 = f32[1,64,8192]{2,0,1:T(1,128)} reshape(f32[1,32,2,8192]{3,2,0,1:T(2,128)} %get-tuple-element.7) | data formatting | bytes 4194304 | tf_op jit(solution)/shard_map/squeeze | solution.py:32
  137.6 3.6 %concatenate.54 = f32[64,8192]{1,0:T(8,128)} reshape(f32[1,32,2,8192]{3,2,0,1:T(2,128)} %get-tuple-element.7) | data formatting | bytes 4194304 | tf_op jit(solution)/shard_map/concatenate | solution.py:33
  141.3 0.0 copy-start.3
  141.3 12.4 %pad_maximum_fusion = f32[1,128,8192]{2,0,1:T(1,128)} fusion(f32[1,64,8192]{2,0,1:T(1,128)} %squeeze.9, f32[1,64,8192]{2,0,1:T(1,128)} %squeeze.8), kind=kLoop, calls=%fused_computation.8 | loop fusion | flops 1048576 | bytes 8388608 | tf_op jit(solution)/shard_map/concatenate | solution.py:33
  153.6 0.0 copy-done.3
  153.6 9.6 %fusion.16 = f32[1,128,128]{2,1,0:T(8,128)} fusion(f32[1,128,8192]{2,0,1:T(1,128)} %pad_maximum_fusion, f32[64,8192]{1,0:T(8,128)} %concatenate.54, f32[64,8192]{1,0:T(8,128)} %concatenate.53, f32[8192]{0:T(1024)S(1)} %copy-done.3), kind=kOutput, calls=%fused_computation.24 | convolution fusion | flops 1612726272 | bytes 8486912 | tf_op jit(solution)/shard_map/fip,fjp->fij/dot_general | solution.py:35
  163.2 0.0 all-reduce.2.cloned.1.call-update
  163.3 0.7 iota_compare_fusion.4
  163.9 110.4 %all-reduce.2.cloned.1.call-done = f32[1,128,128]{2,1,0:T(8,128)} async-done(((f32[1,128,128]{2,1,0:T(8,128)}), f32[1,128,128]{2,1,0:T(8,128)}) %all-reduce.2.cloned.1.call-update) | async-done | bytes 65552 | tf_op jit(solution)/shard_map/psum | solution.py:102
  274.3 1.5 fusion.34
  275.9 0.7 fusion.19
  276.6 0.1 maximum_bitcast_fusion
  277.3 0.0 copy-start.1
  277.3 0.2 fusion.12
  277.5 0.2 fusion.29
  277.7 0.2 fusion.20
  277.9 0.2 fusion.11
  278.1 0.2 fusion.38
  278.3 0.2 fusion.37
  278.6 0.2 fusion.10
  278.8 0.2 fusion.40
  279.0 0.2 fusion.39
  279.2 0.2 fusion.9
  279.4 0.2 convolution_bitcast_fusion
  279.6 0.0 copy-done.1
  279.6 0.0 copy-start.2
  279.6 2.2 fusion.22
  281.8 0.0 copy-done.2
  281.8 1.9 fusion.21
  283.7 2.0 fusion.1
  285.8 3.0 %fusion = bf16[1,1,64,8192]{3,2,1,0:T(8,128)(2,1)} fusion(f32[64,8192]{1,0:T(8,128)S(1)} %fusion.21, f32[64,8192]{1,0:T(8,128)S(1)} %copy-done.1, f32[1,128,128]{2,1,0:T(8,128)S(1)} %convolution_bitcast_fusion), kind=kOutput, calls=%fused_computation.1 | convolution fusion | flops 403701760 | bytes 5275648 | tf_op jit(solution)/shard_map/fij,fip->fjp/dot_general | solution.py:82
  289.4 3.0 fusion.5
  (2 shorter events, 0.1 us)
Async XLA Ops:
  7.2 2.2 copy-start
  15.3 10.8 %copy-start.4 = (s32[32]{0:T(128)S(1)}, s32[32]{0:T(128)}, u32[]{:S(2)}) copy-start(s32[32]{0:T(128)} %param.7) | copy-start | bytes 388
  15.3 103.4 %all-to-all-start = ((f32[2,32,2,8192]{3,2,0,1:T(2,128)}), f32[2,32,2,8192]{3,2,0,1:T(2,128)}, u32[]{:S(2)}, u32[]{:S(2)}) async-start(f32[2,32,2,8192]{3,2,0,1:T(2,128)} %copy.10), calls=%async_computation | async-start | bytes 8388608 | tf_op jit(solution)/shard_map/all_to_all | solution.py:100
  26.1 248.3 %all-reduce.2.cloned.1.call-start = ((), (), s32[]{:S(2)}) async-start(), calls=%async_computation.1 | async-start | bytes 131072 | tf_op jit(solution)/shard_map/psum | solution.py:102
  141.3 12.4 %copy-start.3 = (f32[8192]{0:T(1024)S(1)}, f32[8192]{0:T(1024)}, u32[]{:S(2)}) copy-start(f32[8192]{0:T(1024)} %param.5) | copy-start | bytes 98308
  277.3 2.3 copy-start.1
  279.6 2.2 copy-start.2
Sparse Core Ops, SparseCore 0:
  163.4 110.9 all-reduce.1
where the time goes:
time: 301 us; the launch traced here: 300 us
  waiting for transfers between devices  202 us (67%)
  local copies, waits for them, and re-layouts  28.4 us (9%)
  matrix products  21.6 us (7%)
  other arithmetic  19.8 us (7%)
  between operations  17.4 us (6%)
  starting transfers between devices  10.8 us (4%)
    psum x1, waiting for transfers between devices, shards(): summed = lax.psum(partial_value, 'space')  110 us
    all_to_all x1, waiting for transfers between devices, shards(): lax.all_to_all(spectra, 'tm', split_axis=1, concat_axis=2, tiled=True)  92 us
    concatenate x1, other arithmetic, gram_terms(): stacked = jnp.concatenate([spectra_re, spectra_im], axis=1)  12.4 us
    all_to_all x1, starting transfers between devices, shards(): lax.all_to_all(spectra, 'tm', split_axis=1, concat_axis=2, tiled=True)  10.7 us
    dot_general x1, matrix products, gram_terms(): jnp.einsum('fip,fjp->fij', stacked * point_weights[None, None, :], stacke...  9.63 us
    concatenate x2, local copies, waits for them, and re-layouts, gram_terms(): stacked = jnp.concatenate([spectra_re, spectra_im], axis=1)  7.32 us
  transfers between devices with their start and end apart: 2, of which 2 were waited for; matrix products, arithmetic and copies ran while one was open for 0% of the time, Pallas kernels for 0%

commit v1 on v0

--- a/solution.py
+++ b/solution.py
@@ -99,7 +99,10 @@
     spectra = transform_blocks(dft_table, data, freq_count)
     regrouped = lax.all_to_all(spectra, "tm", split_axis=1, concat_axis=2, tiled=True)
     partial_value = gram_terms(regrouped, weights, total_points)
-    summed = lax.psum(partial_value, "space")
+    peers, summed = (lax.axis_size("space"), partial_value)
+    for far in [1 << k for k in range(peers.bit_length() - 1)]:
+        swap = [(i, i ^ far) for i in range(peers)]
+        summed = summed + lax.ppermute(summed, "space", swap)
     kept_counts = lax.dynamic_slice_in_dim(n_keep, lax.axis_index("tm"), 1)
     mode_field, energy = finish_modes(regrouped, summed, kept_counts, block_count)
     return (mode_field, energy)

time: 301 us -> 203 us (0.67)
  waiting for transfers between devices: 202 us -> 4.84 us
  blocking collectives: 0 us -> 102 us
  starting transfers between devices: 10.8 us -> 25.2 us
  between operations: 17.4 us -> 3.98 us
  local copies, waits for them, and re-layouts: 28.4 us -> 24 us
    psum x1 -> x0, waiting for transfers between devices: 110 us -> none  [shards(): summed = lax.psum(partial_value, 'space')]
    all_to_all x0 -> x1, blocking collectives: none -> 102 us  [shards(): lax.all_to_all(spectra, 'tm', split_axis=1, concat_axis=2, tiled=True)]
    all_to_all x1 -> x0, waiting for transfers between devices: 92 us -> none  [shards(): lax.all_to_all(spectra, 'tm', split_axis=1, concat_axis=2, tiled=True)]
    ppermute x0 -> x4, starting transfers between devices: none -> 25.2 us  [shards(): summed = summed + lax.ppermute(summed, 'space', swap)]
    all_to_all x1 -> x0, starting transfers between devices: 10.7 us -> none  [shards(): lax.all_to_all(spectra, 'tm', split_axis=1, concat_axis=2, tiled=True)]
    ppermute x0 -> x4, waiting for transfers between devices: none -> 4.84 us  [shards(): summed = summed + lax.ppermute(summed, 'space', swap)]
  transfers between devices with their start and end apart: 2 -> 4, of which waited for: 2 -> 4; matrix products, arithmetic and copies ran while one was open for 0% -> 1% of each run, Pallas kernels for 0% -> 0%
where the time goes in v1:
time: 203 us; the launch traced here: 200 us
  blocking collectives  102 us (50%)
  starting transfers between devices  25.2 us (12%)
  local copies, waits for them, and re-layouts  24 us (12%)
  matrix products  20.8 us (10%)
  other arithmetic  19 us (9%)
  waiting for transfers between devices  4.84 us (2%)
  between operations  3.98 us (2%)
    all_to_all x1, blocking collectives, shards(): lax.all_to_all(spectra, 'tm', split_axis=1, concat_axis=2, tiled=True)  102 us
    ppermute x4, starting transfers between devices, shards(): summed = summed + lax.ppermute(summed, 'space', swap)  25.2 us
    concatenate x1, other arithmetic, gram_terms(): stacked = jnp.concatenate([spectra_re, spectra_im], axis=1)  12.3 us
    dot_general x1, matrix products, gram_terms(): jnp.einsum('fip,fjp->fij', stacked * point_weights[None, None, :], stacke...  9.01 us
    concatenate x2, local copies, waits for them, and re-layouts, gram_terms(): stacked = jnp.concatenate([spectra_re, spectra_im], axis=1)  7.33 us
    squeeze x1, local copies, waits for them, and re-layouts, gram_terms(): spectra_re = spectra[0]  5.28 us
    squeeze x1, local copies, waits for them, and re-layouts, gram_terms(): spectra_im = spectra[1]  5.23 us
    ppermute x4, waiting for transfers between devices, shards(): summed = summed + lax.ppermute(summed, 'space', swap)  4.84 us
  transfers between devices with their start and end apart: 4, of which 4 were waited for; matrix products, arithmetic and copies ran while one was open for 1% of the time, Pallas kernels for 0%

profile of v1, /device:TPU:1, one launch (start us, length us, event | category | flops | bytes accessed | tf_op | source)
XLA Modules:
  0.0 199.9 jit_solution(16664004244936908399)
XLA Ops:
  0.6 0.0 copy-start
  0.7 0.7 multiply_reduce_fusion
  2.0 0.8 divide_convert_fusion.1
  2.9 0.0 copy-done
  2.9 0.7 fusion.36
  3.6 3.2 %copy.10 = f32[2,32,2,8192]{3,2,0,1:T(2,128)S(1)} copy(f32[2,32,2,8192]{3,1,2,0:T(8,128)S(1)} %fusion.36) | data formatting | bytes 8388608 | tf_op jit(solution)/shard_map/rt,btp->rbp/dot_general | solution.py:26
  6.8 102.2 %all_to_all.4 = f32[2,32,2,8192]{3,2,0,1:T(2,128)S(1)} all-to-all(f32[2,32,2,8192]{3,2,0,1:T(2,128)S(1)} %copy.10), channel_id=1, replica_groups=mesh['tm'=32,'space'=16] {'tm'}, dimensions={1} | all-to-all | bytes 8388608 | tf_op jit(solution)/shard_map/all_to_all | solution.py:100
  109.0 2.3 %fusion.35 = (f32[1,32,2,8192]{3,2,0,1:T(2,128)}, f32[1,32,2,8192]{3,2,0,1:T(2,128)}) fusion(f32[2,32,2,8192]{3,2,0,1:T(2,128)S(1)} %all_to_all.4), kind=kLoop, calls=%fused_computation.61 | loop fusion | bytes 8388608 | tf_op jit(solution)/shard_map/slice | solution.py:31
  111.3 5.3 %squeeze.8 = f32[1,64,8192]{2,0,1:T(1,128)} reshape(f32[1,32,2,8192]{3,2,0,1:T(2,128)} %get-tuple-element.6) | data formatting | bytes 4194304 | tf_op jit(solution)/shard_map/squeeze | solution.py:31
  116.6 3.7 %concatenate.53 = f32[64,8192]{1,0:T(8,128)} reshape(f32[1,32,2,8192]{3,2,0,1:T(2,128)} %get-tuple-element.6) | data formatting | bytes 4194304 | tf_op jit(solution)/shard_map/concatenate | solution.py:33
  120.2 5.2 %squeeze.9 = f32[1,64,8192]{2,0,1:T(1,128)} reshape(f32[1,32,2,8192]{3,2,0,1:T(2,128)} %get-tuple-element.7) | data formatting | bytes 4194304 | tf_op jit(solution)/shard_map/squeeze | solution.py:32
  125.5 3.6 %concatenate.54 = f32[64,8192]{1,0:T(8,128)} reshape(f32[1,32,2,8192]{3,2,0,1:T(2,128)} %get-tuple-element.7) | data formatting | bytes 4194304 | tf_op jit(solution)/shard_map/concatenate | solution.py:33
  129.1 12.3 %pad_maximum_fusion = f32[1,128,8192]{2,0,1:T(1,128)} fusion(f32[1,64,8192]{2,0,1:T(1,128)} %squeeze.9, f32[1,64,8192]{2,0,1:T(1,128)} %squeeze.8), kind=kLoop, calls=%fused_computation.8 | loop fusion | flops 1048576 | bytes 8388608 | tf_op jit(solution)/shard_map/concatenate | solution.py:33
  141.5 0.0 copy-done.3
  141.5 9.0 %fusion.16 = f32[1,128,128]{2,1,0:T(8,128)S(1)} fusion(f32[1,128,8192]{2,0,1:T(1,128)} %pad_maximum_fusion, f32[64,8192]{1,0:T(8,128)} %concatenate.54, f32[64,8192]{1,0:T(8,128)} %concatenate.53, f32[8192]{0:T(1024)S(1)} %copy-done.3), kind=kOutput, calls=%fused_computation.24 | convolution fusion | flops 1612726272 | bytes 8486912 | tf_op jit(solution)/shard_map/fip,fjp->fij/dot_general | solution.py:35
  150.5 7.1 %collective-permute-start = (f32[1,128,128]{2,1,0:T(8,128)S(1)}, f32[1,128,128]{2,1,0:T(8,128)S(1)}, u32[]{:S(2)}, u32[]{:S(2)}) collective-permute-start(f32[1,128,128]{2,1,0:T(8,128)S(1)} %fusion.16), channel_id=1, source_target_pairs={{0,1},{1,0},{2,3},{3,2},{4,5},{5,4},{6,7},{7,6},{8,9},{9,8},{10,11... | collective-permute-start | bytes 196616 | tf_op jit(solution)/shard_map/ppermute | solution.py:105
  157.6 0.9 collective-permute-done
  158.5 4.0 %collective-permute-start.1 = (f32[1,128,128]{2,1,0:T(8,128)S(1)}, f32[1,128,128]{2,1,0:T(8,128)S(1)}, u32[]{:S(2)}, u32[]{:S(2)}) collective-permute-start(f32[1,128,128]{2,1,0:T(8,128)S(1)} %add.34), channel_id=1, source_target_pairs={{0,2},{1,3},{2,0},{3,1},{4,6},{5,7},{6,4},{7,5},{8,10},{9,11},{10,... | collective-permute-start | bytes 196616 | tf_op jit(solution)/shard_map/ppermute | solution.py:105
  162.5 2.1 %collective-permute-done.1 = f32[1,128,128]{2,1,0:T(8,128)S(1)} collective-permute-done((f32[1,128,128]{2,1,0:T(8,128)S(1)}, f32[1,128,128]{2,1,0:T(8,128)S(1)}, u32[]{:S(2)}, u32[]{:S(2)}) %collective-permute-start.1) | collective-permute-done | bytes 65568 | tf_op jit(solution)/shard_map/ppermute | solution.py:105
  164.6 5.8 %collective-permute-start.2 = (f32[1,128,128]{2,1,0:T(8,128)S(1)}, f32[1,128,128]{2,1,0:T(8,128)S(1)}, u32[]{:S(2)}, u32[]{:S(2)}) collective-permute-start(f32[1,128,128]{2,1,0:T(8,128)S(1)} %add.35), channel_id=1, source_target_pairs={{0,4},{1,5},{2,6},{3,7},{4,0},{5,1},{6,2},{7,3},{8,12},{9,13},{10,... | collective-permute-start | bytes 196616 | tf_op jit(solution)/shard_map/ppermute | solution.py:105
  170.5 0.0 copy-done.4
  170.5 0.6 dynamic_slice.3
  171.1 1.0 collective-permute-done.2
  172.1 8.2 %collective-permute-start.3 = (f32[1,128,128]{2,1,0:T(8,128)S(1)}, f32[1,128,128]{2,1,0:T(8,128)S(1)}, u32[]{:S(2)}, u32[]{:S(2)}) collective-permute-start(f32[1,128,128]{2,1,0:T(8,128)S(1)} %add.36), channel_id=1, source_target_pairs={{0,8},{1,9},{2,10},{3,11},{4,12},{5,13},{6,14},{7,15},{8,0},{9,1},... | collective-permute-start | bytes 196616 | tf_op jit(solution)/shard_map/ppermute | solution.py:105
  180.3 0.7 iota_compare_fusion.4
  181.0 0.8 collective-permute-done.3
  181.8 0.7 fusion.34
  182.5 0.7 fusion.19
  183.2 0.1 maximum_bitcast_fusion
  183.9 0.0 copy-start.1
  183.9 0.2 fusion.12
  184.1 0.2 fusion.29
  184.3 0.2 fusion.20
  184.5 0.2 fusion.11
  184.7 0.2 fusion.38
  184.9 0.2 fusion.37
  185.1 0.2 fusion.10
  185.3 0.2 fusion.40
  185.5 0.2 fusion.39
  185.8 0.2 fusion.9
  186.0 0.2 convolution_bitcast_fusion
  186.2 0.0 copy-done.1
  186.2 0.0 copy-start.2
  186.2 1.9 fusion.22
  188.1 1.9 fusion.21
  190.1 2.0 %fusion.1 = bf16[1,1,64,8192]{3,2,1,0:T(8,128)(2,1)S(1)} fusion(f32[64,8192]{1,0:T(8,128)S(1)} %fusion.22, f32[64,8192]{1,0:T(8,128)S(1)} %copy-done.2, f32[1,128,128]{2,1,0:T(8,128)S(1)} %convolution_bitcast_fusion), kind=kOutput, calls=%fused_computation.3 | convolution fusion | flops 403701760 | bytes 5275648 | tf_op jit(solution)/shard_map/fij,fip->fjp/dot_general | solution.py:79
  192.1 3.0 %fusion = bf16[1,1,64,8192]{3,2,1,0:T(8,128)(2,1)} fusion(f32[64,8192]{1,0:T(8,128)S(1)} %fusion.21, f32[64,8192]{1,0:T(8,128)S(1)} %copy-done.1, f32[1,128,128]{2,1,0:T(8,128)S(1)} %convolution_bitcast_fusion), kind=kOutput, calls=%fused_computation.1 | convolution fusion | flops 403701760 | bytes 5275648 | tf_op jit(solution)/shard_map/fij,fip->fjp/dot_general | solution.py:82
  195.8 3.0 %fusion.5 = bf16[1,2,64,8192]{3,2,1,0:T(8,128)(2,1)} fusion(bf16[1,1,64,8192]{3,2,1,0:T(8,128)(2,1)} %fusion, bf16[1,1,64,8192]{3,2,1,0:T(8,128)(2,1)S(1)} %fusion.1, pred[64]{0:T(512)(128)(4,1)S(1)} %iota_compare_fusion.4), kind=kLoop, calls=%fused_computation.10 | loop fusion | flops 5242880 | bytes 4194368 | tf_op jit(solution)/shard_map/convert_element_type | solution.py:87
  (9 shorter events, 0.1 us)
Async XLA Ops:
  0.6 2.2 %copy-start = (bf16[128,8192]{1,0:T(8,128)(2,1)S(1)}, bf16[128,8192]{1,0:T(8,128)(2,1)}, u32[]{:S(2)}) copy-start(bf16[128,8192]{1,0:T(8,128)(2,1)} %param.4) | copy-start | bytes 6291460
  129.1 12.3 %copy-start.3 = (f32[8192]{0:T(1024)S(1)}, f32[8192]{0:T(1024)}, u32[]{:S(2)}) copy-start(f32[8192]{0:T(1024)} %param.5) | copy-start | bytes 98308
  141.5 29.0 %copy-start.4 = (s32[32]{0:T(128)S(1)}, s32[32]{0:T(128)}, u32[]{:S(2)}) copy-start(s32[32]{0:T(128)} %param.7) | copy-start | bytes 388
  150.5 8.0 %collective-permute-start = (f32[1,128,128]{2,1,0:T(8,128)S(1)}, f32[1,128,128]{2,1,0:T(8,128)S(1)}, u32[]{:S(2)}, u32[]{:S(2)}) collective-permute-start(f32[1,128,128]{2,1,0:T(8,128)S(1)} %fusion.16), channel_id=1, source_target_pairs={{0,1},{1,0},{2,3},{3,2},{4,5},{5,4},{6,7},{7,6},{8,9},{9,8},{10,11... | collective-permute-start | bytes 196616 | tf_op jit(solution)/shard_map/ppermute | solution.py:105
  158.5 6.1 %collective-permute-start.1 = (f32[1,128,128]{2,1,0:T(8,128)S(1)}, f32[1,128,128]{2,1,0:T(8,128)S(1)}, u32[]{:S(2)}, u32[]{:S(2)}) collective-permute-start(f32[1,128,128]{2,1,0:T(8,128)S(1)} %add.34), channel_id=1, source_target_pairs={{0,2},{1,3},{2,0},{3,1},{4,6},{5,7},{6,4},{7,5},{8,10},{9,11},{10,... | collective-permute-start | bytes 196616 | tf_op jit(solution)/shard_map/ppermute | solution.py:105
  164.6 7.5 %collective-permute-start.2 = (f32[1,128,128]{2,1,0:T(8,128)S(1)}, f32[1,128,128]{2,1,0:T(8,128)S(1)}, u32[]{:S(2)}, u32[]{:S(2)}) collective-permute-start(f32[1,128,128]{2,1,0:T(8,128)S(1)} %add.35), channel_id=1, source_target_pairs={{0,4},{1,5},{2,6},{3,7},{4,0},{5,1},{6,2},{7,3},{8,12},{9,13},{10,... | collective-permute-start | bytes 196616 | tf_op jit(solution)/shard_map/ppermute | solution.py:105
  172.1 9.7 %collective-permute-start.3 = (f32[1,128,128]{2,1,0:T(8,128)S(1)}, f32[1,128,128]{2,1,0:T(8,128)S(1)}, u32[]{:S(2)}, u32[]{:S(2)}) collective-permute-start(f32[1,128,128]{2,1,0:T(8,128)S(1)} %add.36), channel_id=1, source_target_pairs={{0,8},{1,9},{2,10},{3,11},{4,12},{5,13},{6,14},{7,15},{8,0},{9,1},... | collective-permute-start | bytes 196616 | tf_op jit(solution)/shard_map/ppermute | solution.py:105
  183.9 2.3 %copy-start.1 = (f32[64,8192]{1,0:T(8,128)S(1)}, f32[64,8192]{1,0:T(8,128)}, u32[]{:S(2)}) copy-start(f32[64,8192]{1,0:T(8,128)} %concatenate.53) | copy-start | bytes 6291460
  186.2 1.9 copy-start.2
